TPU v7x, 256 devices: a whole 4x4x8 slice. The times are simulated.
256 devices in a mesh: req: 8 (over z), exp: 8 (over y, core), hid: 4 (over x).
Axes of the slice: x: 4, y: 4, z: 8, core: 2. Of those that a mesh axis runs over, the one named last changes fastest.
Arguments:
- layer_input_rows: bfloat16 [16384, 1536], P(('req', 'exp')), may hold values from -6 to 6
- attention_norm_gain: float32 [1536], replicated
- query_weight: bfloat16 [1536, 1536], P(None, 'hid'), may hold values from -1 to 1
- key_weight: bfloat16 [1536, 512], P(None, 'hid'), may hold values from -1 to 1
- value_weight: bfloat16 [1536, 512], P(None, 'hid'), may hold values from -0.15625 to 0.15625
- attention_output_weight: bfloat16 [1536, 1536], P('hid'), may hold values from -0.15625 to 0.15625
- query_down_factor: bfloat16 [64, 1536, 16], P(('req', 'exp')), may hold values from -0.15625 to 0.15625
- query_up_factor: bfloat16 [64, 16, 1536], P(('req', 'exp')), may hold values from -1.5 to 1.5
- value_down_factor: bfloat16 [64, 1536, 16], P(('req', 'exp')), may hold values from -0.15625 to 0.15625
- value_up_factor: bfloat16 [64, 16, 512], P(('req', 'exp')), may hold values from -1.5 to 1.5
- lengths: int32 [8, 4], P('req'), may hold values from 1 to 1024, 2048 in all within a row
- request_adapter: int32 [8, 4], replicated, may hold values from 0 to 63
- adapter_home_row: int32 [64], replicated, may hold values from 0 to 63, each once
- expert_norm_gain: float32 [1536], replicated, may hold values from 0.4 to 1.6
- routes: int32 [16384, 8], P(('req', 'exp', 'hid')), may hold values from 0 to 39, all different within a row; in each aligned block of 64 rows (0 to 63, 64 to 127, ...) at most 16 rows name the same one
- router_expert_weight: float32 [16384, 8], P(('req', 'exp', 'hid')), may hold values from 0.1 to 0.5
- expert_gate_weight: bfloat16 [40, 1536, 512], P('exp', None, 'hid'), may hold values from -0.15625 to 0.15625
- expert_up_weight: bfloat16 [40, 1536, 512], P('exp', None, 'hid'), may hold values from -0.15625 to 0.15625
- expert_down_weight: bfloat16 [40, 512, 1536], P('exp', 'hid'), may hold values from -0.25 to 0.25
Outputs:
- attn_out: bfloat16 [16384, 1536], P(('req', 'exp', 'hid'))
- expert_out: bfloat16 [16384, 1536], P(('req', 'exp', 'hid'))
Inputs may be any that keep to these rules, and one draw needn't show every extreme that they name: `lengths`: each row sums to 2048; its largest entry is exactly 1024. `adapter_home_row`: each adapter row appears once. `routes`: A row names 8 different experts. In the rows of one device (64 consecutive rows, aligned) no expert is named more than 16 times, a bound that some block reaches in some of them.
All inputs are finite; a program needn't handle non-finite values.
Results may differ from a plain program's by a relative error of at most 0.029.
The roundings to bfloat16 on the way count: a program that leaves them out, or rounds other values in their place, can miss the bound.
Values may be sent and summed in bfloat16 or wider, within the bound.
No kernel may reach another device: no remote copies, remote signals or barrier semaphores. Data moves between devices by JAX's collectives and lax.ppermute only.
A program may use at most 128 MiB of HBM per device.

v0:
```python
import jax
import jax.numpy as jnp
from jax import lax
from jax.sharding import PartitionSpec as P

HEAD_WIDTH = 64
scale_attn = 0.015625
residual_mult = 0.22
norm_eps = 1e-06
rope_base = 10000.0
neg_large = -1e30


def rms_norm(values, norm_gain):
    widened = values.astype(jnp.float32)
    mean_sq = jnp.mean(widened * widened, axis=-1, keepdims=True)
    return (widened * lax.rsqrt(mean_sq + norm_eps) * norm_gain).astype(jnp.bfloat16)


def rotary(heads_in, position):
    half_size = heads_in.shape[-1] // 2
    frequency = rope_base ** (-2.0 * jnp.arange(half_size, dtype=jnp.float32) / heads_in.shape[-1])
    angles = position.astype(jnp.float32)[:, None] * frequency[None, :]
    cosine = jnp.cos(angles)[:, None, :]
    sine_part = jnp.sin(angles)[:, None, :]
    first_half = heads_in[..., :half_size]
    second_half = heads_in[..., half_size:]
    return jnp.concatenate(
        [
            first_half * cosine - second_half * sine_part,
            second_half * cosine + first_half * sine_part,
        ],
        axis=-1,
    )


def request_of(row_ids, group_len):
    request_end = jnp.cumsum(group_len)
    return jnp.sum((row_ids[:, None] >= request_end[None, :]).astype(jnp.int32), axis=1)


def locate(row_ids, group_len):
    request_end = jnp.cumsum(group_len)
    request_start = request_end - group_len
    request = request_of(row_ids, group_len)
    member = request[:, None] == jnp.arange(group_len.shape[0], dtype=jnp.int32)[None, :]
    position = row_ids - jnp.sum(jnp.where(member, request_start[None, :], 0), axis=1)
    return (request, member, position)


def expert_rows(rows_in, expert_gate_weight, expert_up_weight, expert_down_weight):
    gate_act = jnp.einsum(
        "red,edf->ref", rows_in, expert_gate_weight, preferred_element_type=jnp.float32
    )
    upper = jnp.einsum(
        "red,edf->ref", rows_in, expert_up_weight, preferred_element_type=jnp.float32
    )
    hidden = (jax.nn.silu(gate_act) * upper).astype(jnp.bfloat16)
    return jnp.einsum(
        "ref,efd->red", hidden, expert_down_weight, preferred_element_type=jnp.float32
    )


def per_device(
    layer_input_rows,
    attention_norm_gain,
    query_weight,
    key_weight,
    value_weight,
    attention_output_weight,
    query_down_factor,
    query_up_factor,
    value_down_factor,
    value_up_factor,
    lengths,
    request_adapter,
    adapter_home_row,
    expert_norm_gain,
    routes,
    router_expert_weight,
    expert_gate_weight,
    expert_up_weight,
    expert_down_weight,
):
    exp_count = lax.axis_size("exp")
    hid_count = lax.axis_size("hid")
    exp_index = lax.axis_index("exp")
    hid_index = lax.axis_index("hid")
    req_index = lax.axis_index("req")
    query_rows = layer_input_rows.shape[0]
    width = layer_input_rows.shape[1]
    kv_local = key_weight.shape[1] // HEAD_WIDTH
    q_local = query_weight.shape[1] // HEAD_WIDTH
    group_share = q_local // kv_local
    adapter_rank_size = query_down_factor.shape[2]
    requests = lengths.shape[1]
    group_len = lengths[0]
    row_ids = exp_index * query_rows + jnp.arange(query_rows, dtype=jnp.int32)
    request, member, position = locate(row_ids, group_len)
    wanted = lax.dynamic_index_in_dim(request_adapter, req_index, 0, keepdims=False)
    slot_ids = jnp.arange(adapter_home_row.shape[0], dtype=jnp.int32)
    home_of = jnp.sum(
        jnp.where(wanted[:, None] == slot_ids[None, :], adapter_home_row[None, :], 0), axis=1
    )
    pieces = (
        lax.all_gather(query_down_factor, ("req", "exp"), axis=0, tiled=True),
        lax.all_gather(query_up_factor, ("req", "exp"), axis=0, tiled=True),
        lax.all_gather(value_down_factor, ("req", "exp"), axis=0, tiled=True),
        lax.all_gather(value_up_factor, ("req", "exp"), axis=0, tiled=True),
    )
    adapter_bank_rows = jnp.arange(pieces[0].shape[0], dtype=jnp.int32)
    selector = (home_of[:, None] == adapter_bank_rows[None, :]).astype(jnp.bfloat16)
    picked_now = tuple(
        (
            jnp.einsum("jn,nab->jab", selector, piece_in, preferred_element_type=jnp.float32)
            for piece_in in pieces
        )
    )
    chosen = tuple((fresh for fresh in picked_now))
    qa_sel, qb_sel, va_sel, vb_sel = [member_in.astype(jnp.bfloat16) for member_in in chosen]
    normed_rows = rms_norm(layer_input_rows, attention_norm_gain)

    def low_rank_term(a_sel, b_sel, width_cols, offset):
        inner_terms = jnp.einsum(
            "td,jdr->tjr", normed_rows, a_sel, preferred_element_type=jnp.float32
        )
        inner_terms = (
            jnp.where(member[:, :, None], inner_terms, 0.0)
            .reshape(query_rows, requests * adapter_rank_size)
            .astype(jnp.bfloat16)
        )
        right_factor = lax.dynamic_slice_in_dim(b_sel, offset, width_cols, 2).reshape(
            requests * adapter_rank_size, width_cols
        )
        return jnp.dot(inner_terms, right_factor, preferred_element_type=jnp.float32)

    query_cols = q_local * HEAD_WIDTH
    kv_cols = kv_local * HEAD_WIDTH
    query_matrix = jnp.dot(
        normed_rows, query_weight, preferred_element_type=jnp.float32
    ) + low_rank_term(qa_sel, qb_sel, query_cols, hid_index * query_cols)
    query_matrix = rotary(query_matrix.reshape(query_rows, q_local, HEAD_WIDTH), position).astype(
        jnp.bfloat16
    )
    query_matrix = query_matrix.reshape(query_rows, kv_local, group_share, HEAD_WIDTH)
    keys_own = jnp.dot(normed_rows, key_weight, preferred_element_type=jnp.float32)
    keys_own = (
        rotary(keys_own.reshape(query_rows, kv_local, HEAD_WIDTH), position)
        .astype(jnp.bfloat16)
        .reshape(query_rows, kv_cols)
    )
    values_own = jnp.dot(
        normed_rows, value_weight, preferred_element_type=jnp.float32
    ) + low_rank_term(va_sel, vb_sel, kv_cols, hid_index * kv_cols)
    values_own = values_own.astype(jnp.bfloat16)
    running_max = jnp.full((kv_local, group_share, query_rows), neg_large, jnp.float32)
    key_piece = lax.all_gather(keys_own, "exp", axis=0, tiled=True)
    value_piece = lax.all_gather(values_own, "exp", axis=0, tiled=True)
    piece_len = key_piece.shape[0]
    key_ids = jnp.arange(piece_len, dtype=jnp.int32)
    key_request = request_of(key_ids, group_len)
    allowed = (request[:, None] == key_request[None, :]) & (key_ids[None, :] <= row_ids[:, None])
    key_heads = key_piece.reshape(piece_len, kv_local, HEAD_WIDTH)
    value_heads = value_piece.reshape(piece_len, kv_local, HEAD_WIDTH)
    scores = (
        jnp.einsum("qkgh,nkh->kgqn", query_matrix, key_heads, preferred_element_type=jnp.float32)
        * scale_attn
    )
    scores = jnp.where(allowed[None, None], scores, neg_large)
    new_max = jnp.maximum(running_max, jnp.max(scores, axis=-1))
    weights = jnp.where(allowed[None, None], jnp.exp(scores - new_max[..., None]), 0.0)
    running_sum = jnp.sum(weights, axis=-1)
    running_out = jnp.einsum(
        "kgqn,nkh->kgqh",
        weights.astype(jnp.bfloat16),
        value_heads,
        preferred_element_type=jnp.float32,
    )
    running_max, running_sum, running_out = (new_max, running_sum, running_out)
    attended = (running_out / running_sum[..., None]).astype(jnp.bfloat16)
    attended = jnp.transpose(attended, (2, 0, 1, 3)).reshape(query_rows, query_cols)
    tok_rows = query_rows // hid_count
    attn_out = lax.psum_scatter(
        jnp.dot(attended, attention_output_weight, preferred_element_type=jnp.float32).astype(
            jnp.bfloat16
        ),
        "hid",
        scatter_dimension=0,
        tiled=True,
    )
    own_rows = lax.dynamic_slice_in_dim(layer_input_rows, hid_index * tok_rows, tok_rows, 0)
    mixed_rows = own_rows.astype(jnp.float32) + residual_mult * attn_out.astype(jnp.float32)
    normed_moe = rms_norm(mixed_rows, expert_norm_gain)
    local_exp = expert_gate_weight.shape[0]
    expert_count = local_exp * exp_count
    top_count = routes.shape[1]
    capacity = max(2, tok_rows // 4)
    flat_route = routes.reshape(tok_rows * top_count)
    route_hits = (flat_route[:, None] == jnp.arange(expert_count, dtype=jnp.int32)[None, :]).astype(
        jnp.int32
    )
    earlier = jnp.cumsum(route_hits, axis=0) - route_hits
    slot_pos = jnp.sum(earlier * route_hits, axis=1)
    slots = slot_pos * expert_count + flat_route
    slot_table = jnp.arange(capacity * expert_count, dtype=jnp.int32)
    placed = jnp.any(
        slot_table[:, None, None] == slots.reshape(tok_rows, top_count)[None], axis=2
    ).astype(jnp.bfloat16)
    outgoing = jnp.dot(placed, normed_moe, preferred_element_type=jnp.float32).astype(jnp.bfloat16)
    outgoing = outgoing.reshape(capacity, expert_count, width)
    copies = jnp.broadcast_to(
        outgoing.reshape(capacity, exp_count, 1, local_exp, width),
        (capacity, exp_count, hid_count, local_exp, width),
    )
    copies = copies.reshape(capacity, exp_count * hid_count * local_exp, width)
    arrived = lax.all_to_all(copies, ("exp", "hid"), split_axis=1, concat_axis=0, tiled=True)
    partials = expert_rows(
        arrived, expert_gate_weight, expert_up_weight, expert_down_weight
    ).astype(jnp.bfloat16)
    returned = lax.all_to_all(partials, ("exp", "hid"), split_axis=0, concat_axis=1, tiled=True)
    returned = returned.reshape(capacity, exp_count, hid_count, local_exp, width)
    results = jnp.sum(returned.astype(jnp.float32), axis=2).astype(jnp.bfloat16)
    results = results.reshape(capacity * expert_count, width)
    picked = jnp.take(results, slots, axis=0).reshape(tok_rows, top_count, width)
    expert_out = jnp.sum(
        router_expert_weight[:, :, None] * picked.astype(jnp.float32), axis=1
    ).astype(jnp.bfloat16)
    return (attn_out, expert_out)


def solution(mesh):
    in_specs = (
        P(("req", "exp"), None),
        P(),
        P(None, "hid"),
        P(None, "hid"),
        P(None, "hid"),
        P("hid", None),
        P(("req", "exp"), None, None),
        P(("req", "exp"), None, None),
        P(("req", "exp"), None, None),
        P(("req", "exp"), None, None),
        P("req", None),
        P(),
        P(),
        P(),
        P(("req", "exp", "hid"), None),
        P(("req", "exp", "hid"), None),
        P("exp", None, "hid"),
        P("exp", None, "hid"),
        P("exp", "hid", None),
    )
    out_specs = (P(("req", "exp", "hid"), None), P(("req", "exp", "hid"), None))
    return jax.shard_map(
        per_device, mesh=mesh, in_specs=in_specs, out_specs=out_specs, check_vma=False
    )
```

profile of v0, /device:TPU:1, one launch (start us, length us, event | category | flops | bytes accessed | tf_op | source)
XLA Modules:
  0.0 728.0 jit_solution(7659078790844080535)
XLA Ops:
  17.4 17.2 %all_gather.18 = bf16[2048,128]{0,1:T(8,128)(2,1)} all-gather(bf16[256,128]{0,1:T(8,128)(2,1)S(1)} %bitcast.138), channel_id=1, replica_groups=mesh['req'=8,'exp'=8,'hid'=4] {'exp'}, dimensions={0}, use_global_device_ids=true | all-gather | bytes 589824 | tf_op jit(solution)/shard_map/all_gather | solution.py:157
  35.2 56.6 %all-gather.11.cloned.1.call-done = bf16[64,16,512]{2,1,0:T(8,128)(2,1)} async-done(((bf16[1,16,512]{2,1,0:T(8,128)(2,1)}), bf16[64,16,512]{2,1,0:T(8,128)(2,1)}) %all-gather.11.cloned.1.call-update) | async-done | bytes 1048592 | tf_op jit(solution)/shard_map/all_gather | solution.py:109
  94.2 76.1 %all-gather.5.cloned.1.call-done = bf16[64,1536,16]{1,2,0:T(8,128)(2,1)} async-done(((bf16[1,1536,16]{1,2,0:T(8,128)(2,1)}), bf16[64,1536,16]{1,2,0:T(8,128)(2,1)}) %all-gather.5.cloned.1.call-update) | async-done | bytes 3145744 | tf_op jit(solution)/shard_map/all_gather | solution.py:106
  170.3 5.3 fusion.12
  175.6 72.9 %all-gather.7.cloned.1.call-done = bf16[64,16,1536]{2,1,0:T(8,128)(2,1)} async-done(((bf16[1,16,1536]{2,1,0:T(8,128)(2,1)}), bf16[64,16,1536]{2,1,0:T(8,128)(2,1)}) %all-gather.7.cloned.1.call-update) | async-done | bytes 3145744 | tf_op jit(solution)/shard_map/all_gather | solution.py:107
  248.5 5.4 fusion.8
  259.1 7.7 %fusion = (f32[2,3,256]{2,1,0:T(4,128)S(1)}, f32[2,2048,256,3]{2,1,3,0:T(8,128)}) fusion(pred[256,2048]{0,1:T(8,128)(4,1)S(1)} %fusion.18, bf16[2048,2,64,1]{0,2,3,1:T(8,128)(2,1)} %bitcast.136, bf16[256,2,3,32]{0,3,2,1:T(8,128)(2,1)S(1)} %bitcast.144, bf16[256,2,3,32]{0,3,2,1:T(8,128)(2,1)S(1)} %bitcast.143), kind=kOutput, calls=%fused_computation.3 | convolution fusion | flops 412482048 | bytes 13834240 | tf_op jit(solution)/shard_map/qkgh,nkh->kgqn/dot_general | solution.py:166
  267.3 59.3 %all-gather.9.cloned.1.call-done = bf16[64,1536,16]{1,2,0:T(8,128)(2,1)} async-done(((bf16[1,1536,16]{1,2,0:T(8,128)(2,1)}), bf16[64,1536,16]{1,2,0:T(8,128)(2,1)}) %all-gather.9.cloned.1.call-update) | async-done | bytes 3145744 | tf_op jit(solution)/shard_map/all_gather | solution.py:108
  326.6 5.8 fusion.15
  333.6 13.2 %all_gather.23 = bf16[2048,128]{1,0:T(8,128)(2,1)S(1)} all-gather(bf16[256,128]{1,0:T(8,128)(2,1)S(1)} %fusion.33), channel_id=1, replica_groups=mesh['req'=8,'exp'=8,'hid'=4] {'exp'}, dimensions={0}, use_global_device_ids=true | all-gather | bytes 589824 | tf_op jit(solution)/shard_map/all_gather | solution.py:158
  347.0 7.5 %fusion.1 = f32[2,3,256]{2,1,0:T(4,128)S(1)} fusion(f32[2,2048,256,3]{2,1,3,0:T(8,128)} %get-tuple-element.11, f32[2,3,256]{2,1,0:T(4,128)} %broadcast_maximum_fusion, pred[256,2048]{0,1:T(8,128)(4,1)S(1)} %fusion.18), kind=kLoop, calls=%fused_computation.4 | loop fusion | flops 15727104 | bytes 13119488 | tf_op jit(solution)/shard_map/reduce_sum | solution.py:172
  363.0 17.3 %reduce-scatter.2.cloned.1.call-done = bf16[64,1536]{1,0:T(8,128)(2,1)} async-done(((bf16[256,1536]{1,0:T(8,128)(2,1)}), bf16[64,1536]{1,0:T(8,128)(2,1)}) %reduce-scatter.2.cloned.1.call-update) | async-done | bytes 196624 | tf_op jit(solution)/shard_map/reduce_scatter | solution.py:183
  384.4 4.3 broadcast_in_dim.129
  392.8 98.3 %all_to_all.33 = bf16[16,160,1536]{2,0,1:T(8,128)(2,1)S(1)} all-to-all(bf16[16,160,1536]{2,0,1:T(8,128)(2,1)S(1)} %bitcast.131), channel_id=1, replica_groups=mesh['req'=8,'exp'=8,'hid'=4] {'exp','hid'}, dimensions={1} | all-to-all | bytes 15728640 | tf_op jit(solution)/shard_map/all_to_all | solution.py:216
  491.1 3.9 copy.104
  495.0 6.0 convolution_bitcast_fusion.1
  501.0 12.2 %convert_bitcast_fusion = bf16[512,5,1536]{2,0,1:T(8,128)(2,1)} fusion(bf16[5,128,1536]{2,1,0:T(8,128)(2,1)S(1)} %copy-done, bf16[512,5,1536]{2,0,1:T(8,128)(2,1)} %bitcast.134, bf16[5,1536,128]{2,1,0:T(8,128)(2,1)} %param.36, f32[512,5,128]{2,0,1:T(8,128)S(1)} %convolution_bitcast_fusion.1), kind=kOutput, calls=%fused_computation.6 | convolution fusion | flops 2019164160 | bytes 20971520 | tf_op jit(solution)/shard_map/ref,efd->red/dot_general | solution.py:59
  513.2 12.0 %copy.105 = bf16[512,5,1536]{2,1,0:T(8,128)(2,1)} copy(bf16[512,5,1536]{2,0,1:T(8,128)(2,1)} %convert_bitcast_fusion) | data formatting | bytes 15728640 | tf_op jit(solution)/shard_map/convert_element_type | solution.py:219
  525.1 5.6 all-to-all-start.1
  531.6 162.9 %all-to-all-done.1 = bf16[512,5,1536]{2,1,0:T(8,128)(2,1)} async-done(((bf16[512,5,1536]{2,1,0:T(8,128)(2,1)}), bf16[512,5,1536]{2,1,0:T(8,128)(2,1)}, u32[]{:S(2)}, u32[]{:S(2)}) %all-to-all-start.1) | async-done | bytes 7864352 | tf_op jit(solution)/shard_map/all_to_all | solution.py:220
  694.5 10.2 %reduce.1 = bf16[16,8,5,1536]{3,2,0,1:T(8,128)(2,1)} reduce(bf16[16,8,4,5,1536]{4,3,0,2,1:T(8,128)(2,1)} %bitcast.39, bf16[]{:T(256)} %constant.89.clone.1), dimensions={2}, to_apply=%region_14.15 | reduce | flops 2949120 | bytes 9830402 | tf_op jit(solution)/shard_map/reduce_sum | solution.py:222
  704.7 3.9 copy.107
  708.6 4.3 reshape.289
  712.9 5.5 gather_fusion
  (113 shorter events, 40.4 us)
Async XLA Ops:
  7.2 493.8 %copy-start = (bf16[5,128,1536]{2,1,0:T(8,128)(2,1)S(1)}, bf16[5,128,1536]{2,1,0:T(8,128)(2,1)}, u32[]{:S(2)}) copy-start(bf16[5,128,1536]{2,1,0:T(8,128)(2,1)} %param.37) | copy-start | bytes 5898244
  7.2 84.6 %all-gather.11.cloned.1.call-start = ((), (), s32[]{:S(2)}) async-start(), calls=%async_computation.6 | async-start | bytes 1064960 | tf_op jit(solution)/shard_map/all_gather | solution.py:109
  7.9 162.4 %all-gather.5.cloned.1.call-start = ((), (), s32[]{:S(2)}) async-start(), calls=%async_computation.3 | async-start | bytes 3194880 | tf_op jit(solution)/shard_map/all_gather | solution.py:106
  8.7 239.9 %all-gather.7.cloned.1.call-start = ((), (), s32[]{:S(2)}) async-start(), calls=%async_computation.4 | async-start | bytes 3194880 | tf_op jit(solution)/shard_map/all_gather | solution.py:107
  9.4 317.2 %all-gather.9.cloned.1.call-start = ((), (), s32[]{:S(2)}) async-start(), calls=%async_computation.5 | async-start | bytes 3194880 | tf_op jit(solution)/shard_map/all_gather | solution.py:108
  10.0 370.3 %reduce-scatter.2.cloned.1.call-start = ((), (), s32[]{:S(2)}) async-start(), calls=%async_computation.7 | async-start | bytes 983040 | tf_op jit(solution)/shard_map/reduce_scatter | solution.py:183
  12.7 157.6 %copy-start.9 = (s32[4]{0:T(128)}, s32[4]{0:T(128)S(1)}, u32[]{:S(2)}) copy-start(s32[4]{0:T(128)S(1)} %select_reduce_fusion.1) | copy-start | bytes 52
  14.9 20.3 %copy-start.14 = (f32[256]{0:T(256)}, f32[256]{0:T(256)S(1)}, u32[]{:S(2)}) copy-start(f32[256]{0:T(256)S(1)} %add_rsqrt_fusion) | copy-start | bytes 3076
  175.6 78.3 %copy-start.3 = (bf16[256,1536]{1,0:T(8,128)(2,1)S(1)}, bf16[256,1536]{1,0:T(8,128)(2,1)}, u32[]{:S(2)}) copy-start(bf16[256,1536]{1,0:T(8,128)(2,1)} %param.19) | copy-start | bytes 2359300
  248.5 5.5 copy-start.19
  248.5 5.9 copy-start.11
  248.5 6.1 copy-start.17
  259.0 67.5 %copy-start.10 = (s32[4]{0:T(128)S(1)}, s32[4]{0:T(128)}, u32[]{:S(2)}) copy-start(s32[4]{0:T(128)} %copy-done.9) | copy-start | bytes 52
  266.7 65.7 %copy-start.16 = (f32[256]{0:T(256)S(1)}, f32[256]{0:T(256)}, u32[]{:S(2)}) copy-start(f32[256]{0:T(256)} %copy-done.14) | copy-start | bytes 3076
  266.7 65.7 %copy-start.20 = (f32[1536]{0:T(1024)S(1)}, f32[1536]{0:T(1024)}, u32[]{:S(2)}) copy-start(f32[1536]{0:T(1024)} %param.20) | copy-start | bytes 18436
  267.3 65.6 %copy-start.12 = (pred[256,4]{0,1:T(4,128)(4,1)S(1)}, pred[256,4]{0,1:T(4,128)(4,1)}, u32[]{:S(2)}) copy-start(pred[256,4]{0,1:T(4,128)(4,1)} %iota_compare_fusion.5) | copy-start | bytes 3076
  326.6 6.5 copy-start.18
  347.0 8.2 %copy-start.2 = (f32[2,2048,256,3]{2,1,3,0:T(8,128)S(1)}, f32[2,2048,256,3]{2,1,3,0:T(8,128)}, u32[]{:S(2)}) copy-start(f32[2,2048,256,3]{2,1,3,0:T(8,128)} %get-tuple-element.11) | copy-start | bytes 37748740
  347.0 8.2 %copy-start.6 = (f32[2,3,256]{2,1,0:T(4,128)S(1)}, f32[2,3,256]{2,1,0:T(4,128)}, u32[]{:S(2)}) copy-start(f32[2,3,256]{2,1,0:T(4,128)} %broadcast_maximum_fusion) | copy-start | bytes 18436
  358.9 21.5 %copy-start.4 = (bf16[256,1536]{1,0:T(8,128)(2,1)S(1)}, bf16[256,1536]{1,0:T(8,128)(2,1)}, u32[]{:S(2)}) copy-start(bf16[256,1536]{1,0:T(8,128)(2,1)} %param.19) | copy-start | bytes 2359300
  358.9 22.6 %copy-start.8 = (f32[1536]{0:T(1024)S(1)}, f32[1536]{0:T(1024)}, u32[]{:S(2)}) copy-start(f32[1536]{0:T(1024)} %param.32) | copy-start | bytes 18436
  525.1 5.8 copy-start.13
  525.1 169.4 %all-to-all-start.1 = ((bf16[512,5,1536]{2,1,0:T(8,128)(2,1)}), bf16[512,5,1536]{2,1,0:T(8,128)(2,1)}, u32[]{:S(2)}, u32[]{:S(2)}) async-start(bf16[512,5,1536]{2,1,0:T(8,128)(2,1)} %copy.105), calls=%async_computation.2 | async-start | bytes 25165824 | tf_op jit(solution)/shard_map/all_to_all | solution.py:220
  712.9 8.3 %copy-start.1 = (bf16[5,128,1536]{2,1,0:T(8,128)(2,1)S(1)}, bf16[5,128,1536]{2,1,0:T(8,128)(2,1)}, u32[]{:S(2)}) copy-start(bf16[5,128,1536]{2,1,0:T(8,128)(2,1)} %param.37) | copy-start | bytes 5898244
  (3 other events, 10.6 us)
Sparse Core Ops, SparseCore 0:
  10.8 80.9 all-gather.10
  94.6 75.7 all-gather.4
  173.1 75.4 all-gather.6
  251.1 75.4 all-gather.8
  360.5 19.7 reduce-scatter.1
where the time goes:
time: 739 us; the launch traced here: 728 us
  waiting for transfers between devices  448 us (61%)
  blocking collectives  129 us (17%)
  matrix products  57.6 us (8%)
  local copies, waits for them, and re-layouts  43.5 us (6%)
  other arithmetic  30.3 us (4%)
  between operations  14.4 us (2%)
    all_to_all x1, waiting for transfers between devices, per_device(): lax.all_to_all(partials, ('exp', 'hid'), split_axis=0, concat_axis=1, til...  163 us
    all_to_all x1, blocking collectives, per_device(): lax.all_to_all(copies, ('exp', 'hid'), split_axis=1, concat_axis=0, tiled...  98.3 us
    all_gather x1, waiting for transfers between devices, per_device(): lax.all_gather(query_down_factor, ('req', 'exp'), axis=0, tiled=True)  76.1 us
    all_gather x1, waiting for transfers between devices, per_device(): lax.all_gather(query_up_factor, ('req', 'exp'), axis=0, tiled=True)  72.9 us
    all_gather x1, waiting for transfers between devices, per_device(): lax.all_gather(value_down_factor, ('req', 'exp'), axis=0, tiled=True)  59.3 us
    all_gather x1, waiting for transfers between devices, per_device(): lax.all_gather(value_up_factor, ('req', 'exp'), axis=0, tiled=True)  56.6 us
    dot_general x4, matrix products, per_device(): jnp.einsum('jn,nab->jab', selector, piece_in, preferred_element_type=jnp....  18.9 us
    reduce_scatter x1, waiting for transfers between devices, per_device(): lax.psum_scatter(jnp.dot(attended, attention_output_weight, preferred_ele...  17.3 us
  transfers between devices with their start and end apart: 6, of which 6 were waited for; matrix products, arithmetic and copies ran while one was open for 5% of the time, Pallas kernels for 0%

commit v1 on v0

--- a/solution.py
+++ b/solution.py
@@ -217,7 +217,10 @@
     partials = expert_rows(
         arrived, expert_gate_weight, expert_up_weight, expert_down_weight
     ).astype(jnp.bfloat16)
-    returned = lax.all_to_all(partials, ("exp", "hid"), split_axis=0, concat_axis=1, tiled=True)
+    size = lax.axis_size(("exp", "hid"))
+    blocks = jnp.stack(jnp.split(partials, size, axis=0), axis=0)
+    blocks = lax.all_to_all(blocks, ("exp", "hid"), split_axis=0, concat_axis=0)
+    returned = jnp.concatenate(blocks, axis=1)
     returned = returned.reshape(capacity, exp_count, hid_count, local_exp, width)
     results = jnp.sum(returned.astype(jnp.float32), axis=2).astype(jnp.bfloat16)
     results = results.reshape(capacity * expert_count, width)

time: 739 us -> 706 us (0.955)
  waiting for transfers between devices: 448 us -> 374 us
  local copies, waits for them, and re-layouts: 43.5 us -> 84.2 us
    all_to_all x1, waiting for transfers between devices: 163 us -> 91 us  [per_device(): blocks = lax.all_to_all(blocks, ('exp', 'hid'), split_axis=0, concat_axis=0)]
    unnamed x44 -> x63, local copies, waits for them, and re-layouts: 1.6 us -> 53.1 us
    convert_element_type x1 -> x0, local copies, waits for them, and re-layouts: 12 us -> none  [per_device(): partials = expert_rows(arrived, expert_gate_weight, expert_up_weight, exp...]
  transfers between devices with their start and end apart: 6 -> 6, of which waited for: 6 -> 6; matrix products, arithmetic and copies ran while one was open for 5% -> 6% of each run, Pallas kernels for 0% -> 0%
where the time goes in v1:
time: 706 us; the launch traced here: 692 us
  waiting for transfers between devices  374 us (53%)
  blocking collectives  128 us (18%)
  local copies, waits for them, and re-layouts  84.2 us (12%)
  matrix products  61.2 us (9%)
  other arithmetic  24.4 us (3%)
  between operations  14.4 us (2%)
    all_to_all x1, blocking collectives, per_device(): lax.all_to_all(copies, ('exp', 'hid'), split_axis=1, concat_axis=0, tiled...  98 us
    all_to_all x1, waiting for transfers between devices, per_device(): blocks = lax.all_to_all(blocks, ('exp', 'hid'), split_axis=0, concat_axis=0)  91 us
    all_gather x1, waiting for transfers between devices, per_device(): lax.all_gather(query_down_factor, ('req', 'exp'), axis=0, tiled=True)  76.1 us
    all_gather x1, waiting for transfers between devices, per_device(): lax.all_gather(query_up_factor, ('req', 'exp'), axis=0, tiled=True)  72.9 us
    all_gather x1, waiting for transfers between devices, per_device(): lax.all_gather(value_down_factor, ('req', 'exp'), axis=0, tiled=True)  57.3 us
    all_gather x1, waiting for transfers between devices, per_device(): lax.all_gather(value_up_factor, ('req', 'exp'), axis=0, tiled=True)  56.6 us
    unnamed x63, local copies, waits for them, and re-layouts  53.1 us
    dot_general x4, matrix products, per_device(): jnp.einsum('jn,nab->jab', selector, piece_in, preferred_element_type=jnp....  18.8 us
  transfers between devices with their start and end apart: 6, of which 6 were waited for; matrix products, arithmetic and copies ran while one was open for 6% of the time, Pallas kernels for 0%

profile of v1, /device:TPU:1, one launch (start us, length us, event | category | flops | bytes accessed | tf_op | source)
XLA Modules:
  0.0 692.4 jit_solution(7970348818856229289)
XLA Ops:
  17.5 17.2 %all_gather.18 = bf16[2048,128]{0,1:T(8,128)(2,1)} all-gather(bf16[256,128]{0,1:T(8,128)(2,1)S(1)} %bitcast.262), channel_id=1, replica_groups=mesh['req'=8,'exp'=8,'hid'=4] {'exp'}, dimensions={0}, use_global_device_ids=true | all-gather | bytes 589824 | tf_op jit(solution)/shard_map/all_gather | solution.py:157
  35.2 56.6 %all-gather.11.cloned.1.call-done = bf16[64,16,512]{2,1,0:T(8,128)(2,1)} async-done(((bf16[1,16,512]{2,1,0:T(8,128)(2,1)}), bf16[64,16,512]{2,1,0:T(8,128)(2,1)}) %all-gather.11.cloned.1.call-update) | async-done | bytes 1048592 | tf_op jit(solution)/shard_map/all_gather | solution.py:109
  94.2 76.1 %all-gather.5.cloned.1.call-done = bf16[64,1536,16]{1,2,0:T(8,128)(2,1)} async-done(((bf16[1,1536,16]{1,2,0:T(8,128)(2,1)}), bf16[64,1536,16]{1,2,0:T(8,128)(2,1)}) %all-gather.5.cloned.1.call-update) | async-done | bytes 3145744 | tf_op jit(solution)/shard_map/all_gather | solution.py:106
  170.3 5.3 fusion.12
  175.7 72.9 %all-gather.7.cloned.1.call-done = bf16[64,16,1536]{2,1,0:T(8,128)(2,1)} async-done(((bf16[1,16,1536]{2,1,0:T(8,128)(2,1)}), bf16[64,16,1536]{2,1,0:T(8,128)(2,1)}) %all-gather.7.cloned.1.call-update) | async-done | bytes 3145744 | tf_op jit(solution)/shard_map/all_gather | solution.py:107
  248.5 5.3 fusion.8
  261.6 7.7 %fusion = (f32[2,3,256]{2,1,0:T(4,128)S(1)}, f32[2,2048,256,3]{2,1,3,0:T(8,128)}) fusion(pred[256,2048]{0,1:T(8,128)(4,1)S(1)} %fusion.18, bf16[2048,2,64,1]{0,2,3,1:T(8,128)(2,1)} %bitcast.260, bf16[256,2,3,32]{0,3,2,1:T(8,128)(2,1)S(1)} %bitcast.268, bf16[256,2,3,32]{0,3,2,1:T(8,128)(2,1)S(1)} %bitcast.267), kind=kOutput, calls=%fused_computation.3 | convolution fusion | flops 412482048 | bytes 13834240 | tf_op jit(solution)/shard_map/qkgh,nkh->kgqn/dot_general | solution.py:166
  269.3 57.3 %all-gather.9.cloned.1.call-done = bf16[64,1536,16]{1,2,0:T(8,128)(2,1)} async-done(((bf16[1,1536,16]{1,2,0:T(8,128)(2,1)}), bf16[64,1536,16]{1,2,0:T(8,128)(2,1)}) %all-gather.9.cloned.1.call-update) | async-done | bytes 3145744 | tf_op jit(solution)/shard_map/all_gather | solution.py:108
  326.6 5.8 fusion.15
  334.5 13.2 %all_gather.23 = bf16[2048,128]{1,0:T(8,128)(2,1)S(1)} all-gather(bf16[256,128]{1,0:T(8,128)(2,1)S(1)} %fusion.33), channel_id=1, replica_groups=mesh['req'=8,'exp'=8,'hid'=4] {'exp'}, dimensions={0}, use_global_device_ids=true | all-gather | bytes 589824 | tf_op jit(solution)/shard_map/all_gather | solution.py:158
  348.8 7.4 %fusion.1 = f32[2,3,256]{2,1,0:T(4,128)S(1)} fusion(f32[2,2048,256,3]{2,1,3,0:T(8,128)} %get-tuple-element.11, f32[2,3,256]{2,1,0:T(4,128)S(1)} %broadcast_maximum_fusion, pred[256,2048]{0,1:T(8,128)(4,1)S(1)} %fusion.18), kind=kLoop, calls=%fused_computation.4 | loop fusion | flops 15727104 | bytes 13119488 | tf_op jit(solution)/shard_map/reduce_sum | solution.py:172
  357.1 3.6 fusion.39
  364.8 17.6 %reduce-scatter.2.cloned.1.call-done = bf16[64,1536]{1,0:T(8,128)(2,1)} async-done(((bf16[256,1536]{1,0:T(8,128)(2,1)}), bf16[64,1536]{1,0:T(8,128)(2,1)}) %reduce-scatter.2.cloned.1.call-update) | async-done | bytes 196624 | tf_op jit(solution)/shard_map/reduce_scatter | solution.py:183
  386.5 4.3 broadcast_in_dim.129
  390.8 3.2 copy.99
  394.9 98.0 %all_to_all.23 = bf16[16,160,1536]{2,0,1:T(8,128)(2,1)S(1)} all-to-all(bf16[16,160,1536]{2,0,1:T(8,128)(2,1)S(1)} %bitcast.255), channel_id=1, replica_groups=mesh['req'=8,'exp'=8,'hid'=4] {'exp','hid'}, dimensions={1} | all-to-all | bytes 15728640 | tf_op jit(solution)/shard_map/all_to_all | solution.py:216
  492.9 3.9 copy.100
  496.8 6.0 convolution_bitcast_fusion.1
  502.8 12.2 %convert_bitcast_fusion = bf16[512,5,1536]{2,0,1:T(8,128)(2,1)} fusion(bf16[5,128,1536]{2,1,0:T(8,128)(2,1)S(1)} %copy-done, bf16[512,5,1536]{2,0,1:T(8,128)(2,1)} %bitcast.258, bf16[5,1536,128]{2,1,0:T(8,128)(2,1)} %param.36, f32[512,5,128]{2,0,1:T(8,128)S(1)} %convolution_bitcast_fusion.1), kind=kOutput, calls=%fused_computation.7 | convolution fusion | flops 2019164160 | bytes 20971520 | tf_op jit(solution)/shard_map/ref,efd->red/dot_general | solution.py:59
  568.1 5.5 all-to-all-start.1
  574.4 91.0 %all-to-all-done.1 = bf16[32,16,5,1536]{3,1,2,0:T(8,128)(2,1)} async-done(((bf16[32,16,5,1536]{3,1,2,0:T(8,128)(2,1)}), bf16[32,16,5,1536]{3,1,2,0:T(8,128)(2,1)}, u32[]{:S(2)}, u32[]{:S(2)}) %all-to-all-start.1) | async-done | bytes 7864352 | tf_op jit(solution)/shard_map/all_to_all | solution.py:222
  665.5 4.9 bitcast_reduce_fusion
  673.1 4.3 reshape.288
  677.4 5.4 gather_fusion
  (132 shorter events, 93.5 us)
Async XLA Ops:
  7.2 495.6 %copy-start = (bf16[5,128,1536]{2,1,0:T(8,128)(2,1)S(1)}, bf16[5,128,1536]{2,1,0:T(8,128)(2,1)}, u32[]{:S(2)}) copy-start(bf16[5,128,1536]{2,1,0:T(8,128)(2,1)} %param.37) | copy-start | bytes 5898244
  7.2 246.7 %copy-start.2 = (bf16[256,1536]{1,0:T(8,128)(2,1)S(1)}, bf16[256,1536]{1,0:T(8,128)(2,1)}, u32[]{:S(2)}) copy-start(bf16[256,1536]{1,0:T(8,128)(2,1)} %param.19) | copy-start | bytes 2359300
  7.2 84.6 %all-gather.11.cloned.1.call-start = ((), (), s32[]{:S(2)}) async-start(), calls=%async_computation.6 | async-start | bytes 1064960 | tf_op jit(solution)/shard_map/all_gather | solution.py:109
  7.9 162.4 %all-gather.5.cloned.1.call-start = ((), (), s32[]{:S(2)}) async-start(), calls=%async_computation.3 | async-start | bytes 3194880 | tf_op jit(solution)/shard_map/all_gather | solution.py:106
  8.7 239.9 %all-gather.7.cloned.1.call-start = ((), (), s32[]{:S(2)}) async-start(), calls=%async_computation.4 | async-start | bytes 3194880 | tf_op jit(solution)/shard_map/all_gather | solution.py:107
  9.4 317.2 %all-gather.9.cloned.1.call-start = ((), (), s32[]{:S(2)}) async-start(), calls=%async_computation.5 | async-start | bytes 3194880 | tf_op jit(solution)/shard_map/all_gather | solution.py:108
  10.0 372.4 %reduce-scatter.2.cloned.1.call-start = ((), (), s32[]{:S(2)}) async-start(), calls=%async_computation.7 | async-start | bytes 983040 | tf_op jit(solution)/shard_map/reduce_scatter | solution.py:183
  12.7 157.6 %copy-start.8 = (s32[4]{0:T(128)}, s32[4]{0:T(128)S(1)}, u32[]{:S(2)}) copy-start(s32[4]{0:T(128)S(1)} %select_reduce_fusion.1) | copy-start | bytes 52
  14.9 19.8 %copy-start.12 = (f32[256]{0:T(256)}, f32[256]{0:T(256)S(1)}, u32[]{:S(2)}) copy-start(f32[256]{0:T(256)S(1)} %add_rsqrt_fusion) | copy-start | bytes 3076
  258.6 68.0 %copy-start.9 = (s32[4]{0:T(128)S(1)}, s32[4]{0:T(128)}, u32[]{:S(2)}) copy-start(s32[4]{0:T(128)} %copy-done.8) | copy-start | bytes 52
  261.6 70.8 %copy-start.13 = (f32[256]{0:T(256)S(1)}, f32[256]{0:T(256)}, u32[]{:S(2)}) copy-start(f32[256]{0:T(256)} %copy-done.12) | copy-start | bytes 3076
  261.6 70.8 %copy-start.14 = (f32[1536]{0:T(1024)S(1)}, f32[1536]{0:T(1024)}, u32[]{:S(2)}) copy-start(f32[1536]{0:T(1024)} %param.20) | copy-start | bytes 18436
  261.6 71.2 %copy-start.10 = (pred[256,4]{0,1:T(4,128)(4,1)S(1)}, pred[256,4]{0,1:T(4,128)(4,1)}, u32[]{:S(2)}) copy-start(pred[256,4]{0,1:T(4,128)(4,1)} %iota_compare_fusion.5) | copy-start | bytes 3076
  348.8 8.2 %copy-start.1 = (f32[2,2048,256,3]{2,1,3,0:T(8,128)S(1)}, f32[2,2048,256,3]{2,1,3,0:T(8,128)}, u32[]{:S(2)}) copy-start(f32[2,2048,256,3]{2,1,3,0:T(8,128)} %get-tuple-element.11) | copy-start | bytes 37748740
  348.8 8.3 %copy-start.5 = (bf16[2048,128]{0,1:T(8,128)(2,1)S(1)}, bf16[2048,128]{0,1:T(8,128)(2,1)}, u32[]{:S(2)}) copy-start(bf16[2048,128]{0,1:T(8,128)(2,1)} %copy.90) | copy-start | bytes 1572868
  357.0 3.6 copy-start.4
  357.0 5.1 copy-start.6
  357.0 25.4 %copy-start.3 = (bf16[256,1536]{1,0:T(8,128)(2,1)S(1)}, bf16[256,1536]{1,0:T(8,128)(2,1)}, u32[]{:S(2)}) copy-start(bf16[256,1536]{1,0:T(8,128)(2,1)} %param.19) | copy-start | bytes 2359300
  357.1 26.5 %copy-start.7 = (f32[1536]{0:T(1024)S(1)}, f32[1536]{0:T(1024)}, u32[]{:S(2)}) copy-start(f32[1536]{0:T(1024)} %param.32) | copy-start | bytes 18436
  568.1 5.7 copy-start.11
  568.1 97.4 %all-to-all-start.1 = ((bf16[32,16,5,1536]{3,1,2,0:T(8,128)(2,1)}), bf16[32,16,5,1536]{3,1,2,0:T(8,128)(2,1)}, u32[]{:S(2)}, u32[]{:S(2)}) async-start(bf16[32,16,5,1536]{3,1,2,0:T(8,128)(2,1)} %fusion.43), calls=%async_computation.2 | async-start | bytes 15728640 | tf_op jit(solution)/shard_map/all_to_all | solution.py:222
Sparse Core Ops, SparseCore 0:
  10.8 80.9 all-gather.10
  94.6 75.7 all-gather.4
  173.1 75.4 all-gather.6
  251.1 75.4 all-gather.8
  362.3 20.0 reduce-scatter.1
